TPU v7x, 128 devices: a whole 4x4x4 slice. The times are simulated.
128 devices in a mesh: req: 8 (over z, core), exp: 16 (over x, y).
Axes of the slice: x: 4, y: 4, z: 4, core: 2. Of those that a mesh axis runs over, the one named last changes fastest.
Arguments:
- tokens: bfloat16 [32768, 1536], P(('req', 'exp')), may hold values from -6 to 6
- attn_gain: float32 [1536], replicated, may hold values from 0.1 to 1.9
- w_query: bfloat16 [1536, 1536], P('req'), may hold values from -0.15625 to 0.15625
- key_projection: bfloat16 [1536, 256], P('req'), may hold values from -0.15625 to 0.15625
- value_projection: bfloat16 [1536, 256], P('req'), may hold values from -0.15625 to 0.15625
- w_out: bfloat16 [1536, 1536], P(None, 'req'), may hold values from -0.15625 to 0.15625
- moe_gain: float32 [1536], replicated, may hold values from 0.1 to 1.9
- w_gate: bfloat16 [32, 1536, 768], P('exp'), may hold values from -0.15625 to 0.15625
- w_up: bfloat16 [32, 1536, 768], P('exp'), may hold values from -0.15625 to 0.15625
- w_down: bfloat16 [32, 768, 1536], P('exp'), may hold values from -0.21875 to 0.21875
- routes: int32 [32768, 4], P(('req', 'exp')), may hold values from 0 to 31, all different within a row; in each aligned block of 128 rows (0 to 127, 128 to 255, ...) at most 24 rows name the same one
- gate_weights: float32 [32768, 4], P(('req', 'exp')), may hold values from 0.1 to 1
- kv_cache: bfloat16 [512, 1024, 512], P(('req', 'exp')), may hold values from -360 to 360, as said below
- lengths: int32 [512], P(('req', 'exp')), may hold values from 128 to 1024, as said below
- parents: int32 [512, 64], P(('req', 'exp')), may hold values from 0 to 62, as said below
- accepted: int32 [512], P(('req', 'exp')), may hold values from 0 to 63
Outputs:
- layer_out: bfloat16 [32768, 1536], P(('req', 'exp'))
- new_entries: bfloat16 [512, 64, 512], P(('req', 'exp'))
Inputs may be any that keep to these rules, and one draw needn't show every extreme that they name: `routes`: each row names 4 different experts; among the rows of one aligned block of 128 rows no expert is named more than 24 times, and in some block one expert exactly 24 times. `kv_cache`: cache entries are finite; slots at or after a request's length hold arbitrary values. `lengths`: some request has exactly 1024 live slots. parents[r, 0] = 0 marks the root; for i >= 1, parents[r, i] < i.
All inputs are finite; a program needn't handle non-finite values.
Results may differ from a plain program's by a relative error of at most 0.013.
The roundings to bfloat16 on the way count: a program that leaves them out, or rounds other values in their place, can miss the bound.
Values may be sent and summed in bfloat16 or wider, within the bound.
No kernel may reach another device: no remote copies, remote signals or barrier semaphores. Data moves between devices by JAX's collectives and lax.ppermute only.
A program may use at most 128 MiB of HBM per device.

v0:
```python
import math
import jax
import jax.numpy as jnp
from jax import lax
from jax.sharding import PartitionSpec as P

QUERY_HEADS = 12
KEY_VALUE_HEADS = 2
HEAD_SIZE = 128
EXPERTS = 32
TOP = 4
DRAFT_TOKENS = 64
CAP = 24
BLOCK_ROWS = 128
eps_norm = 1e-06
rope_base = 1000000.0


def rms_scale(token_rows, gain_vec):
    widened = token_rows.astype(jnp.float32)
    inverse = lax.rsqrt(jnp.mean(widened * widened, axis=-1, keepdims=True) + eps_norm)
    return (widened * inverse * gain_vec).astype(jnp.bfloat16)


def rotate(values, positions):
    row_count = values.shape[0]
    head_count = values.shape[1] // HEAD_SIZE
    half_size = HEAD_SIZE // 2
    reshaped_rows = values.reshape(row_count, head_count, HEAD_SIZE)
    frequency = rope_base ** (-jnp.arange(half_size, dtype=jnp.float32) / half_size)
    angles = positions.astype(jnp.float32)[:, None] * frequency[None, :]
    cosine = jnp.cos(angles)[:, None, :]
    sine_part = jnp.sin(angles)[:, None, :]
    leading = reshaped_rows[..., :half_size]
    second = reshaped_rows[..., half_size:]
    turned = jnp.concatenate(
        [leading * cosine - second * sine_part, second * cosine + leading * sine_part], axis=-1
    )
    return turned.reshape(row_count, head_count * HEAD_SIZE)


def ancestry(parents):
    node_count = parents.shape[-1]
    node_index = jnp.arange(node_count, dtype=jnp.int32)
    parent_step = (parents[..., :, None] == node_index[None, None, :]).astype(jnp.float32)
    closure = jnp.maximum(parent_step, jnp.eye(node_count, dtype=jnp.float32)[None])
    for squaring in range(max(1, (node_count - 1).bit_length())):
        closure = jnp.minimum(jnp.einsum("rij,rjk->rik", closure, closure), 1.0)
    tree_depth = jnp.sum(closure, axis=-1).astype(jnp.int32) - 1
    return (closure, tree_depth)


def attend(query_rows, tree_key_value, cached_row_block, length, closure):
    tree_drafts = query_rows.shape[0]
    queries_per_group = QUERY_HEADS // KEY_VALUE_HEADS
    key_value_width = KEY_VALUE_HEADS * HEAD_SIZE
    reshaped_rows = query_rows.reshape(tree_drafts, KEY_VALUE_HEADS, queries_per_group, HEAD_SIZE)
    cached_key_rows = cached_row_block[:, :key_value_width].reshape(-1, KEY_VALUE_HEADS, HEAD_SIZE)
    cached_value_rows = cached_row_block[:, key_value_width:].reshape(
        -1, KEY_VALUE_HEADS, HEAD_SIZE
    )
    tree_key_rows = tree_key_value[:, :key_value_width].reshape(-1, KEY_VALUE_HEADS, HEAD_SIZE)
    tree_value_rows = tree_key_value[:, key_value_width:].reshape(-1, KEY_VALUE_HEADS, HEAD_SIZE)
    scale = 1.0 / math.sqrt(HEAD_SIZE)
    cache_scores = (
        jnp.einsum(
            "igsd,jgd->gsij", reshaped_rows, cached_key_rows, preferred_element_type=jnp.float32
        )
        * scale
    )
    draft_scores = (
        jnp.einsum(
            "igsd,jgd->gsij", reshaped_rows, tree_key_rows, preferred_element_type=jnp.float32
        )
        * scale
    )
    live_cache = (jnp.arange(cached_row_block.shape[0]) < length)[None, None, None, :]
    live_draft = (closure > 0.5)[None, None, :, :]
    cache_scores = jnp.where(live_cache, cache_scores, -1e30)
    draft_scores = jnp.where(live_draft, draft_scores, -1e30)
    highest = jnp.maximum(jnp.max(cache_scores, axis=-1), jnp.max(draft_scores, axis=-1))[..., None]
    cache_weight = jnp.exp(cache_scores - highest)
    draft_weight = jnp.exp(draft_scores - highest)
    running = jnp.sum(cache_weight, axis=-1, keepdims=True) + jnp.sum(
        draft_weight, axis=-1, keepdims=True
    )
    cache_probs = (cache_weight / running).astype(jnp.bfloat16)
    draft_probs = (draft_weight / running).astype(jnp.bfloat16)
    context = jnp.einsum(
        "gsij,jgd->igsd", cache_probs, cached_value_rows, preferred_element_type=jnp.float32
    )
    context = context + jnp.einsum(
        "gsij,jgd->igsd", draft_probs, tree_value_rows, preferred_element_type=jnp.float32
    )
    return context.reshape(tree_drafts, QUERY_HEADS * HEAD_SIZE).astype(jnp.bfloat16)


def compact(kv_rows, closure, tree_depth, accepted):
    path_mask = jnp.take_along_axis(closure, accepted[:, None, None], axis=1)[:, 0, :]
    level = jnp.arange(kv_rows.shape[1], dtype=jnp.int32)
    select = (
        path_mask[:, None, :] * (tree_depth[:, None, :] == level[None, :, None]).astype(jnp.float32)
    ).astype(jnp.bfloat16)
    return jnp.einsum("rtj,rjw->rtw", select, kv_rows, preferred_element_type=jnp.float32).astype(
        jnp.bfloat16
    )


def slot_tables(routes, gate_weights, capacity):
    rows = routes.shape[0]
    expert_ids = jnp.arange(EXPERTS, dtype=jnp.int32)
    picks = routes[:, :, None] == expert_ids[None, None, :]
    chosen = jnp.sum(picks.astype(jnp.int32), axis=1).astype(jnp.bfloat16)
    row_ids = jnp.arange(rows, dtype=jnp.int32)
    same_block = row_ids[None, :] // BLOCK_ROWS == row_ids[:, None] // BLOCK_ROWS
    before = ((row_ids[None, :] < row_ids[:, None]) & same_block).astype(jnp.bfloat16)
    earlier = jnp.dot(before, chosen, preferred_element_type=jnp.float32).astype(jnp.int32)
    slot_number = jnp.sum(jnp.where(picks, earlier[:, None, :], 0), axis=2)
    slot_index = routes * capacity + slot_number
    slot_ids = jnp.arange(EXPERTS * capacity, dtype=jnp.int32)
    hit = slot_index[:, :, None] == slot_ids[None, None, :]
    place = jnp.sum(hit.astype(jnp.bfloat16), axis=1)
    weight = jnp.sum(jnp.where(hit, gate_weights[:, :, None], 0.0), axis=1)
    weight_hi = weight.astype(jnp.bfloat16)
    weight_lo = (weight - weight_hi.astype(jnp.float32)).astype(jnp.bfloat16)
    return (place, weight_hi, weight_lo)


def pack_slots(token_rows, place):
    return jnp.einsum("ts,td->sd", place, token_rows, preferred_element_type=jnp.bfloat16)


def expert_products(received, w_gate, w_up, w_down):
    gate_part = jnp.einsum("pekd,edf->pekf", received, w_gate, preferred_element_type=jnp.float32)
    up_part = jnp.einsum("pekd,edf->pekf", received, w_up, preferred_element_type=jnp.float32)
    hidden = (jnp.maximum(gate_part, 0.0) * up_part).astype(jnp.bfloat16)
    return jnp.einsum("pekf,efd->pekd", hidden, w_down, preferred_element_type=jnp.float32).astype(
        jnp.bfloat16
    )


def combine_picks(returned_rows, weight_hi, weight_lo):
    layer_width = returned_rows.shape[-1]
    rows = weight_hi.shape[0]
    flat_rows = returned_rows.reshape(-1, layer_width)
    both = jnp.concatenate([weight_hi, weight_lo], axis=0)
    mixed = jnp.dot(both, flat_rows, preferred_element_type=jnp.float32)
    return mixed[:rows] + mixed[rows:]


def routed_whole(moe_in, place, weight_hi, weight_lo, w_gate, w_up, w_down):
    capacity = place.shape[1] // EXPERTS
    buffer = pack_slots(moe_in, place)
    peer_count = lax.axis_size("exp")
    reshaped_rows = buffer.reshape(peer_count, w_gate.shape[0], capacity, moe_in.shape[1])
    produced = expert_products(
        lax.all_to_all(reshaped_rows, "exp", split_axis=0, concat_axis=0, tiled=True),
        w_gate,
        w_up,
        w_down,
    )
    returned_rows = lax.all_to_all(produced, "exp", split_axis=0, concat_axis=0, tiled=True)
    return combine_picks(returned_rows, weight_hi, weight_lo)


def local(
    tokens,
    attn_gain,
    w_query,
    key_projection,
    value_projection,
    w_out,
    moe_gain,
    w_gate,
    w_up,
    w_down,
    routes,
    gate_weights,
    kv_cache,
    lengths,
    parents,
    accepted,
):
    rows_here = tokens.shape[0]
    local_reqs = kv_cache.shape[0]
    normed = rms_scale(tokens, attn_gain)
    closure, tree_depth = ancestry(parents)
    positions = (lengths[:, None] + tree_depth).reshape(-1)
    query_sum = jnp.dot(
        normed,
        lax.all_gather(w_query, "req", axis=0, tiled=True),
        preferred_element_type=jnp.float32,
    )
    key_sum = jnp.dot(
        normed,
        lax.all_gather(key_projection, "req", axis=0, tiled=True),
        preferred_element_type=jnp.float32,
    )
    value_sum = jnp.dot(
        normed,
        lax.all_gather(value_projection, "req", axis=0, tiled=True),
        preferred_element_type=jnp.float32,
    )
    query_rows = rotate(query_sum, positions).astype(jnp.bfloat16)
    tree_key_value = jnp.concatenate([rotate(key_sum, positions), value_sum], axis=1).astype(
        jnp.bfloat16
    )
    query_req = query_rows.reshape(local_reqs, DRAFT_TOKENS, query_rows.shape[1])
    key_value_request = tree_key_value.reshape(local_reqs, DRAFT_TOKENS, tree_key_value.shape[1])
    w_out_full = lax.all_gather(w_out, "req", axis=1, tiled=True)
    chunk_count = rows_here // BLOCK_ROWS
    context_all = jax.vmap(attend)(
        query_req, key_value_request, kv_cache, lengths, closure
    ).reshape(rows_here, -1)
    place, weight_hi, weight_lo = slot_tables(routes, gate_weights, CAP)
    outs = []
    for chunk in range(chunk_count):
        rw = slice(chunk * BLOCK_ROWS, (chunk + 1) * BLOCK_ROWS)
        attn_out = jnp.dot(context_all[rw], w_out_full, preferred_element_type=jnp.float32)
        residual = (tokens[rw].astype(jnp.float32) + attn_out).astype(jnp.bfloat16)
        moe_in = rms_scale(residual, moe_gain)
        mixed = routed_whole(moe_in, place[rw], weight_hi[rw], weight_lo[rw], w_gate, w_up, w_down)
        outs.append((residual.astype(jnp.float32) + mixed).astype(jnp.bfloat16))
    layer_out = jnp.concatenate(outs, axis=0)
    new_entries = compact(key_value_request, closure, tree_depth, accepted)
    return (layer_out, new_entries)


def solution(mesh):
    return jax.shard_map(
        local,
        mesh=mesh,
        in_specs=(
            P(("req", "exp"), None),
            P(),
            P("req", None),
            P("req", None),
            P("req", None),
            P(None, "req"),
            P(),
            P("exp", None, None),
            P("exp", None, None),
            P("exp", None, None),
            P(("req", "exp"), None),
            P(("req", "exp"), None),
            P(("req", "exp"), None, None),
            P(("req", "exp")),
            P(("req", "exp"), None),
            P(("req", "exp")),
        ),
        out_specs=(P(("req", "exp"), None), P(("req", "exp"), None, None)),
        check_vma=False,
    )
```

profile of v0, /device:TPU:0, one launch (start us, length us, event | category | flops | bytes accessed | tf_op | source)
XLA Modules:
  0.0 250.2 jit_solution(5174756153162118243)
XLA Ops:
  13.0 15.6 %all_gather.13 = bf16[1536,256]{1,0:T(8,128)(2,1)S(1)} all-gather(bf16[192,256]{1,0:T(8,128)(2,1)S(1)} %copy-done.16), channel_id=1, replica_groups=mesh['req'=8,'exp'=16] {'req'}, dimensions={0}, use_global_device_ids=true | all-gather | bytes 884736 | tf_op jit(solution)/shard_map/all_gather | solution.py:196
  30.2 4.6 %fusion.137 = (bf16[4,1024,256]{2,1,0:T(8,128)(2,1)}, bf16[4,1024,256]{2,1,0:T(8,128)(2,1)}) fusion(bf16[4,1024,512]{2,1,0:T(8,128)(2,1)} %param.28), kind=kLoop, calls=%fused_computation.165 | loop fusion | bytes 8388608 | tf_op jit(solution)/shard_map/vmap()/slice | solution.py:59
  34.8 3.0 %copy.161 = bf16[4,1024,256]{1,2,0:T(8,128)(2,1)S(1)} copy(bf16[4,1024,256]{2,1,0:T(8,128)(2,1)} %get-tuple-element.5) | data formatting | bytes 4194304
  37.8 15.3 %all_gather.14 = bf16[1536,256]{1,0:T(8,128)(2,1)S(1)} all-gather(bf16[192,256]{1,0:T(8,128)(2,1)} %param.20), channel_id=1, replica_groups=mesh['req'=8,'exp'=16] {'req'}, dimensions={0}, use_global_device_ids=true | all-gather | bytes 884736 | tf_op jit(solution)/shard_map/all_gather | solution.py:201
  56.5 4.0 %copy.164 = bf16[4,1024,256]{1,2,0:T(8,128)(2,1)} copy(bf16[4,1024,256]{2,1,0:T(8,128)(2,1)} %get-tuple-element.4) | data formatting | bytes 4194304
  62.6 4.4 %fusion.135 = f32[256,1536]{0,1:T(8,128)S(1)} fusion(bf16[1536,1536]{1,0:T(8,128)(2,1)} %all-gather.3.cloned.1.call-done, bf16[256,1536]{1,0:T(8,128)(2,1)S(1)} %copy-done.2, f32[1536]{0:T(1024)} %param.17, f32[256]{0:T(256)} %copy-done.21), kind=kOutput, calls=%fused_computation.164 | convolution fusion | flops 1209532416 | bytes 7085056 | tf_op jit(solution)/shard_map/dot_general | solution.py:189
  73.1 3.1 %fusion.1 = f32[4,2,6,64]{3,2,1,0:T(8,128)S(1)} fusion(f32[4,2,64,6,1024]{4,2,3,1,0:T(8,128)S(1)} %get-tuple-element.25, f32[4,2,6,64]{3,2,1,0:T(8,128)S(1)} %max.25, pred[4,1024]{1,0:T(4,128)(4,1)S(1)} %iota_compare_fusion.8), kind=kLoop, calls=%fused_computation.6 | loop fusion | flops 12579840 | bytes 12611584 | tf_op jit(solution)/shard_map/vmap()/reduce_sum | solution.py:84
  77.8 3.9 %fusion.40 = bf16[4,64,2,6,128]{4,1,3,2,0:T(8,128)(2,1)S(1)} fusion(f32[4,2,128,6,64]{2,4,3,1,0:T(8,128)S(1)} %fusion.74, bf16[4,1024,2,128,1]{1,3,4,2,0:T(8,128)(2,1)S(1)} %bitcast.120, f32[4,2,64,6,1024]{4,2,3,1,0:T(8,128)S(1)} %get-tuple-element.25, f32[4,2,6,64]{3,2,1,0:T(8,128)S(1)} %add.113, f32[4,2,6,64]{3,2,1,0:T(8,128)S(1)} %max.25, ...), kind=kOutput, calls=%fused_computation.46 | convolution fusion | flops 821821440 | bytes 17068032 | tf_op jit(solution)/shard_map/vmap(gsij,jgd->igsd)/dot_general | solution.py:89
  84.3 4.1 %multiply_reduce_fusion.1 = (f32[128]{0:T(128)S(1)}, f32[128,1536]{1,0:T(8,128)S(1)}) fusion(bf16[128,1536]{1,0:T(8,128)(2,1)S(1)} %slice.78, bf16[1536,1536]{0,1:T(8,128)(2,1)} %all-gather.5.cloned.1.call-done, bf16[256,1536]{1,0:T(8,128)(2,1)S(1)} %copy-done.3), kind=kOutput, calls=%fused_computation.75 | convolution fusion | flops 605159296 | bytes 6291968 | tf_op jit(solution)/shard_map/dot_general | solution.py:219
  90.7 6.9 %all-to-all-start = ((bf16[16,2,24,1536]{3,2,1,0:T(8,128)(2,1)}), bf16[16,2,24,1536]{3,2,1,0:T(8,128)(2,1)}, u32[]{:S(2)}, u32[]{:S(2)}) async-start(bf16[16,2,24,1536]{3,2,1,0:T(8,128)(2,1)} %bitcast.14), calls=%async_computation | async-start | bytes 4718592 | tf_op jit(solution)/shard_map/all_to_all | solution.py:157
  98.3 4.1 %multiply_reduce_fusion = (f32[128]{0:T(128)S(1)}, f32[128,1536]{1,0:T(8,128)S(1)}) fusion(bf16[128,1536]{1,0:T(8,128)(2,1)S(1)} %slice.86, bf16[1536,1536]{0,1:T(8,128)(2,1)} %all-gather.5.cloned.1.call-done, bf16[256,1536]{1,0:T(8,128)(2,1)S(1)} %copy-done.3), kind=kOutput, calls=%fused_computation.73 | convolution fusion | flops 605159296 | bytes 6291968 | tf_op jit(solution)/shard_map/dot_general | solution.py:219
  105.5 25.7 %all-to-all-done = bf16[16,2,24,1536]{3,2,1,0:T(8,128)(2,1)} async-done(((bf16[16,2,24,1536]{3,2,1,0:T(8,128)(2,1)}), bf16[16,2,24,1536]{3,2,1,0:T(8,128)(2,1)}, u32[]{:S(2)}, u32[]{:S(2)}) %all-to-all-start) | async-done | bytes 2359328 | tf_op jit(solution)/shard_map/all_to_all | solution.py:157
  131.2 5.3 %all-to-all-start.2 = ((bf16[16,2,24,1536]{3,2,1,0:T(8,128)(2,1)}), bf16[16,2,24,1536]{3,2,1,0:T(8,128)(2,1)S(1)}, u32[]{:S(2)}, u32[]{:S(2)}) async-start(bf16[16,2,24,1536]{3,2,1,0:T(8,128)(2,1)} %bitcast.24), calls=%async_computation.2 | async-start | bytes 4718592 | tf_op jit(solution)/shard_map/all_to_all | solution.py:157
  136.6 6.5 %fusion.9 = f32[2,16,24,768]{3,2,1,0:T(8,128)} fusion(bf16[2,1536,768]{2,1,0:T(8,128)(2,1)} %param.24, bf16[16,2,24,1536]{3,2,1,0:T(8,128)(2,1)} %all-to-all-done), kind=kOutput, calls=%fused_computation.14 | convolution fusion | flops 1811939328 | bytes 9437184 | tf_op jit(solution)/shard_map/pekd,edf->pekf/dot_general | solution.py:135
  143.1 10.4 %fusion.25 = bf16[16,2,24,1536]{3,2,0,1:T(8,128)(2,1)} fusion(bf16[2,768,1536]{2,1,0:T(8,128)(2,1)} %param.25, f32[2,16,24,768]{3,2,1,0:T(8,128)} %fusion.9, bf16[2,1536,768]{2,1,0:T(8,128)(2,1)} %param.23, bf16[16,2,24,1536]{3,2,1,0:T(8,128)(2,1)} %all-to-all-done), kind=kOutput, calls=%fused_computation.26 | convolution fusion | flops 3626827776 | bytes 16515072 | tf_op jit(solution)/shard_map/pekf,efd->pekd/dot_general | solution.py:137
  153.5 3.4 %copy.136 = bf16[16,2,24,1536]{3,2,1,0:T(8,128)(2,1)} copy(bf16[16,2,24,1536]{3,2,0,1:T(8,128)(2,1)} %fusion.25) | data formatting | bytes 4718592 | tf_op jit(solution)/shard_map/convert_element_type | solution.py:137
  156.9 12.0 %all-to-all-done.2 = bf16[16,2,24,1536]{3,2,1,0:T(8,128)(2,1)S(1)} async-done(((bf16[16,2,24,1536]{3,2,1,0:T(8,128)(2,1)}), bf16[16,2,24,1536]{3,2,1,0:T(8,128)(2,1)S(1)}, u32[]{:S(2)}, u32[]{:S(2)}) %all-to-all-start.2) | async-done | bytes 2359328 | tf_op jit(solution)/shard_map/all_to_all | solution.py:157
  170.3 4.0 %all-to-all-start.1 = ((bf16[16,2,24,1536]{3,2,1,0:T(8,128)(2,1)}), bf16[16,2,24,1536]{3,2,1,0:T(8,128)(2,1)S(1)}, u32[]{:S(2)}, u32[]{:S(2)}) async-start(bf16[16,2,24,1536]{3,2,1,0:T(8,128)(2,1)} %copy.136), calls=%async_computation.1 | async-start | bytes 4718592 | tf_op jit(solution)/shard_map/all_to_all | solution.py:162
  176.1 6.5 %fusion.7 = f32[2,16,24,768]{3,2,1,0:T(8,128)} fusion(bf16[2,1536,768]{2,1,0:T(8,128)(2,1)} %param.24, bf16[16,2,24,1536]{3,2,1,0:T(8,128)(2,1)} %copy-done.4), kind=kOutput, calls=%fused_computation.12 | convolution fusion | flops 1811939328 | bytes 9437184 | tf_op jit(solution)/shard_map/pekd,edf->pekf/dot_general | solution.py:135
  182.6 10.4 %fusion.22 = bf16[16,2,24,1536]{3,2,0,1:T(8,128)(2,1)} fusion(bf16[2,768,1536]{2,1,0:T(8,128)(2,1)} %param.25, f32[2,16,24,768]{3,2,1,0:T(8,128)} %fusion.7, bf16[2,1536,768]{2,1,0:T(8,128)(2,1)} %param.23, bf16[16,2,24,1536]{3,2,1,0:T(8,128)(2,1)} %copy-done.4), kind=kOutput, calls=%fused_computation.25 | convolution fusion | flops 3626827776 | bytes 16515072 | tf_op jit(solution)/shard_map/pekf,efd->pekd/dot_general | solution.py:137
  193.0 3.4 %copy.140 = bf16[16,2,24,1536]{3,2,1,0:T(8,128)(2,1)} copy(bf16[16,2,24,1536]{3,2,0,1:T(8,128)(2,1)} %fusion.22) | data formatting | bytes 4718592 | tf_op jit(solution)/shard_map/convert_element_type | solution.py:137
  196.4 8.2 %all-to-all-done.1 = bf16[16,2,24,1536]{3,2,1,0:T(8,128)(2,1)S(1)} async-done(((bf16[16,2,24,1536]{3,2,1,0:T(8,128)(2,1)}), bf16[16,2,24,1536]{3,2,1,0:T(8,128)(2,1)S(1)}, u32[]{:S(2)}, u32[]{:S(2)}) %all-to-all-start.1) | async-done | bytes 2359328 | tf_op jit(solution)/shard_map/all_to_all | solution.py:162
  204.6 4.7 %all-to-all-start.3 = ((bf16[16,2,24,1536]{3,2,1,0:T(8,128)(2,1)}), bf16[16,2,24,1536]{3,2,1,0:T(8,128)(2,1)}, u32[]{:S(2)}, u32[]{:S(2)}) async-start(bf16[16,2,24,1536]{3,2,1,0:T(8,128)(2,1)} %copy.140), calls=%async_computation.3 | async-start | bytes 4718592 | tf_op jit(solution)/shard_map/all_to_all | solution.py:162
  211.7 28.1 %all-to-all-done.3 = bf16[16,2,24,1536]{3,2,1,0:T(8,128)(2,1)} async-done(((bf16[16,2,24,1536]{3,2,1,0:T(8,128)(2,1)}), bf16[16,2,24,1536]{3,2,1,0:T(8,128)(2,1)}, u32[]{:S(2)}, u32[]{:S(2)}) %all-to-all-start.3) | async-done | bytes 2359328 | tf_op jit(solution)/shard_map/all_to_all | solution.py:162
  (119 shorter events, 38.0 us)
Async XLA Ops:
  7.2 5.6 %copy-start.2 = (bf16[256,1536]{1,0:T(8,128)(2,1)S(1)}, bf16[256,1536]{1,0:T(8,128)(2,1)}, u32[]{:S(2)}) copy-start(bf16[256,1536]{1,0:T(8,128)(2,1)} %param.16) | copy-start | bytes 2359300
  7.2 5.8 %copy-start.16 = (bf16[192,256]{1,0:T(8,128)(2,1)S(1)}, bf16[192,256]{1,0:T(8,128)(2,1)}, u32[]{:S(2)}) copy-start(bf16[192,256]{1,0:T(8,128)(2,1)} %param.19) | copy-start | bytes 294916
  7.2 21.4 %copy-start.22 = (f32[1536]{0:T(1024)S(1)}, f32[1536]{0:T(1024)}, u32[]{:S(2)}) copy-start(f32[1536]{0:T(1024)} %param.17) | copy-start | bytes 18436
  7.2 55.4 %all-gather.3.cloned.1.call-start = ((), (), s32[]{:S(2)}) async-start(), calls=%async_computation.4 | async-start | bytes 5308416 | tf_op jit(solution)/shard_map/all_gather | solution.py:191
  7.9 76.4 %all-gather.5.cloned.1.call-start = ((), (), s32[]{:S(2)}) async-start(), calls=%async_computation.5 | async-start | bytes 5308416 | tf_op jit(solution)/shard_map/all_gather | solution.py:210
  11.9 17.3 %copy-start.8 = (f32[256,64]{0,1:T(8,128)}, f32[256,64]{0,1:T(8,128)S(1)}, u32[]{:S(2)}) copy-start(f32[256,64]{0,1:T(8,128)S(1)} %get-tuple-element.20) | copy-start | bytes 196612
  11.9 17.3 %copy-start.10 = (f32[256,64]{0,1:T(8,128)}, f32[256,64]{0,1:T(8,128)S(1)}, u32[]{:S(2)}) copy-start(f32[256,64]{0,1:T(8,128)S(1)} %get-tuple-element.21) | copy-start | bytes 196612
  13.0 40.1 %copy-start.21 = (f32[256]{0:T(256)}, f32[256]{0:T(256)S(1)}, u32[]{:S(2)}) copy-start(f32[256]{0:T(256)S(1)} %add_rsqrt_fusion) | copy-start | bytes 3076
  54.9 5.7 %copy-start.17 = (s32[256,4]{0,1:T(4,128)S(1)}, s32[256,4]{0,1:T(4,128)}, u32[]{:S(2)}) copy-start(s32[256,4]{0,1:T(4,128)} %param.26) | copy-start | bytes 12292
  56.5 6.0 %copy-start.20 = (s32[4]{0:T(128)S(1)}, s32[4]{0:T(128)}, u32[]{:S(2)}) copy-start(s32[4]{0:T(128)} %param.29) | copy-start | bytes 52
  61.7 8.0 %copy-start.6 = (bf16[256,2,128]{2,0,1:T(8,128)(2,1)}, bf16[256,2,128]{2,0,1:T(8,128)(2,1)S(1)}, u32[]{:S(2)}) copy-start(bf16[256,2,128]{2,0,1:T(8,128)(2,1)S(1)} %pad_maximum_fusion.2) | copy-start | bytes 393220
  62.6 4.4 %copy-start.9 = (f32[256,64]{0,1:T(8,128)S(1)}, f32[256,64]{0,1:T(8,128)}, u32[]{:S(2)}) copy-start(f32[256,64]{0,1:T(8,128)} %copy-done.8) | copy-start | bytes 196612
  62.6 4.5 %copy-start.11 = (f32[256,64]{0,1:T(8,128)S(1)}, f32[256,64]{0,1:T(8,128)}, u32[]{:S(2)}) copy-start(f32[256,64]{0,1:T(8,128)} %copy-done.10) | copy-start | bytes 196612
  73.1 3.1 %copy-start.15 = (bf16[4,64,2,128]{3,2,1,0:T(2,128)(2,1)S(1)}, bf16[4,64,2,128]{3,2,1,0:T(2,128)(2,1)}, u32[]{:S(2)}) copy-start(bf16[4,64,2,128]{3,2,1,0:T(2,128)(2,1)} %reshape.304) | copy-start | bytes 393220
  82.6 5.8 %copy-start.18 = (f32[1536]{0:T(1024)S(1)}, f32[1536]{0:T(1024)}, u32[]{:S(2)}) copy-start(f32[1536]{0:T(1024)} %param.22) | copy-start | bytes 18436
  90.7 40.5 %all-to-all-start = ((bf16[16,2,24,1536]{3,2,1,0:T(8,128)(2,1)}), bf16[16,2,24,1536]{3,2,1,0:T(8,128)(2,1)}, u32[]{:S(2)}, u32[]{:S(2)}) async-start(bf16[16,2,24,1536]{3,2,1,0:T(8,128)(2,1)} %bitcast.14), calls=%async_computation | async-start | bytes 4718592 | tf_op jit(solution)/shard_map/all_to_all | solution.py:157
  131.2 37.6 %all-to-all-start.2 = ((bf16[16,2,24,1536]{3,2,1,0:T(8,128)(2,1)}), bf16[16,2,24,1536]{3,2,1,0:T(8,128)(2,1)S(1)}, u32[]{:S(2)}, u32[]{:S(2)}) async-start(bf16[16,2,24,1536]{3,2,1,0:T(8,128)(2,1)} %bitcast.24), calls=%async_computation.2 | async-start | bytes 4718592 | tf_op jit(solution)/shard_map/all_to_all | solution.py:157
  156.9 17.4 %copy-start.7 = (bf16[256,2,128]{2,0,1:T(8,128)(2,1)S(1)}, bf16[256,2,128]{2,0,1:T(8,128)(2,1)}, u32[]{:S(2)}) copy-start(bf16[256,2,128]{2,0,1:T(8,128)(2,1)} %copy-done.6) | copy-start | bytes 393220
  156.9 17.7 %copy-start.23 = (s32[4]{0:T(128)S(1)}, s32[4]{0:T(128)}, u32[]{:S(2)}) copy-start(s32[4]{0:T(128)} %param.31) | copy-start | bytes 52
  170.3 34.3 %all-to-all-start.1 = ((bf16[16,2,24,1536]{3,2,1,0:T(8,128)(2,1)}), bf16[16,2,24,1536]{3,2,1,0:T(8,128)(2,1)S(1)}, u32[]{:S(2)}, u32[]{:S(2)}) async-start(bf16[16,2,24,1536]{3,2,1,0:T(8,128)(2,1)} %copy.136), calls=%async_computation.1 | async-start | bytes 4718592 | tf_op jit(solution)/shard_map/all_to_all | solution.py:162
  196.4 12.9 %copy-start.19 = (f32[256,4]{0,1:T(4,128)S(1)}, f32[256,4]{0,1:T(4,128)}, u32[]{:S(2)}) copy-start(f32[256,4]{0,1:T(4,128)} %param.27) | copy-start | bytes 12292
  196.4 13.3 %copy-start.14 = (bf16[256,256]{1,0:T(8,128)(2,1)S(1)}, bf16[256,256]{1,0:T(8,128)(2,1)}, u32[]{:S(2)}) copy-start(bf16[256,256]{1,0:T(8,128)(2,1)} %convolution_convert_fusion.1) | copy-start | bytes 393220
  204.6 35.2 %all-to-all-start.3 = ((bf16[16,2,24,1536]{3,2,1,0:T(8,128)(2,1)}), bf16[16,2,24,1536]{3,2,1,0:T(8,128)(2,1)}, u32[]{:S(2)}, u32[]{:S(2)}) async-start(bf16[16,2,24,1536]{3,2,1,0:T(8,128)(2,1)} %copy.140), calls=%async_computation.3 | async-start | bytes 4718592 | tf_op jit(solution)/shard_map/all_to_all | solution.py:162
  211.7 30.6 %copy-start.1 = (f32[128,1536]{1,0:T(8,128)S(1)}, f32[128,1536]{1,0:T(8,128)}, u32[]{:S(2)}) copy-start(f32[128,1536]{1,0:T(8,128)} %copy-done) | copy-start | bytes 2359300
  (6 other events, 9.7 us)
Sparse Core Ops, SparseCore 0:
  9.7 38.5 all-gather.2
  50.0 34.2 all-gather.4
where the time goes:
time: 251 us; the launch traced here: 250 us
  waiting for transfers between devices  77 us (31%)
  matrix products  67 us (27%)
  blocking collectives  30.9 us (12%)
  local copies, waits for them, and re-layouts  30.2 us (12%)
  starting transfers between devices  21 us (8%)
  between operations  14.6 us (6%)
  other arithmetic  9.53 us (4%)
    all_to_all x2, waiting for transfers between devices, routed_whole(): lax.all_to_all(reshaped_rows, 'exp', split_axis=0, concat_axis=0, tiled=T...  37.7 us
    all_to_all x2, waiting for transfers between devices, routed_whole(): lax.all_to_all(produced, 'exp', split_axis=0, concat_axis=0, tiled=True)  36.3 us
    dot_general x2, matrix products, expert_products(): jnp.einsum('pekf,efd->pekd', hidden, w_down, preferred_element_type=jnp.f...  20.8 us
    all_gather x1, blocking collectives, local(): lax.all_gather(key_projection, 'req', axis=0, tiled=True)  15.6 us
    all_gather x1, blocking collectives, local(): lax.all_gather(value_projection, 'req', axis=0, tiled=True)  15.3 us
    dot_general x2, matrix products, expert_products(): jnp.einsum('pekd,edf->pekf', received, w_up, preferred_element_type=jnp.f...  13 us
    all_to_all x2, starting transfers between devices, routed_whole(): lax.all_to_all(reshaped_rows, 'exp', split_axis=0, concat_axis=0, tiled=T...  12.2 us
    unnamed x53, local copies, waits for them, and re-layouts  10.8 us
  transfers between devices with their start and end apart: 6, of which 5 were waited for; matrix products, arithmetic and copies ran while one was open for 37% of the time, Pallas kernels for 0%

commit v1 on v0

--- a/solution.py
+++ b/solution.py
@@ -14,6 +14,33 @@
 BLOCK_ROWS = 128
 eps_norm = 1e-06
 rope_base = 1000000.0
+
+
+def replace_members_all_now(message, row_dim):
+    u_next = list(message.shape[1:])
+    u_next[row_dim] *= message.shape[0]
+    return jnp.moveaxis(message, 0, row_dim).reshape(u_next)
+
+
+def wrap_bench(which_dim, mat, mesh_name):
+    cores_n = jax.lax.axis_size(mesh_name)
+    pool = [(kk, (kk + 1) % cores_n) for kk in range(cores_n)]
+    found = [(dev, w) for w, dev in pool]
+    fresh, p_next = ([], [])
+    hop_no = 0
+    while hop_no < cores_n - 1:
+        if hop_no % 2 == 0:
+            fresh.append(jax.lax.ppermute(fresh[-1] if fresh else mat, mesh_name, pool))
+        else:
+            met_up = jax.lax.ppermute(p_next[-1] if p_next else mat, mesh_name, found)
+            p_next.append(met_up)
+        hop_no = hop_no + 1
+    s_next = jnp.stack([*fresh[::-1], mat, *p_next])
+    y_new = jax.lax.axis_index(mesh_name)
+    d_next = len(fresh)
+    b_now = y_new - d_next
+    s_next = s_next[(jnp.arange(cores_n) - b_now) % cores_n]
+    return replace_members_all_now(s_next, which_dim)
 
 
 def rms_scale(token_rows, gain_vec):
@@ -197,9 +224,7 @@
         preferred_element_type=jnp.float32,
     )
     value_sum = jnp.dot(
-        normed,
-        lax.all_gather(value_projection, "req", axis=0, tiled=True),
-        preferred_element_type=jnp.float32,
+        normed, wrap_bench(0, value_projection, "req"), preferred_element_type=jnp.float32
     )
     query_rows = rotate(query_sum, positions).astype(jnp.bfloat16)
     tree_key_value = jnp.concatenate([rotate(key_sum, positions), value_sum], axis=1).astype(

time: 251 us -> 260 us (1.036)
  the two profiles are of different devices: /device:TPU:0 before, /device:TPU:96 now
where the time goes in v1:
time: 260 us; the launch traced here: 259 us
  waiting for transfers between devices  87.5 us (34%)
  matrix products  65.8 us (25%)
  local copies, waits for them, and re-layouts  37.2 us (14%)
  starting transfers between devices  28.5 us (11%)
  between operations  14.7 us (6%)
  blocking collectives  14.6 us (6%)
  other arithmetic  10.5 us (4%)
    all_to_all x2, waiting for transfers between devices, routed_whole(): lax.all_to_all(reshaped_rows, 'exp', split_axis=0, concat_axis=0, tiled=T...  44.1 us
    all_to_all x2, waiting for transfers between devices, routed_whole(): lax.all_to_all(produced, 'exp', split_axis=0, concat_axis=0, tiled=True)  35.5 us
    dot_general x2, matrix products, expert_products(): jnp.einsum('pekf,efd->pekd', hidden, w_down, preferred_element_type=jnp.f...  19.4 us
    unnamed x50, local copies, waits for them, and re-layouts  16.3 us
    all_gather x1, blocking collectives, local(): lax.all_gather(key_projection, 'req', axis=0, tiled=True)  14.6 us
    all_to_all x2, starting transfers between devices, routed_whole(): lax.all_to_all(reshaped_rows, 'exp', split_axis=0, concat_axis=0, tiled=T...  14.3 us
    dot_general x2, matrix products, expert_products(): jnp.einsum('pekd,edf->pekf', received, w_up, preferred_element_type=jnp.f...  13 us
    all_to_all x2, starting transfers between devices, routed_whole(): lax.all_to_all(produced, 'exp', split_axis=0, concat_axis=0, tiled=True)  8.39 us
  transfers between devices with their start and end apart: 13, of which 8 were waited for; matrix products, arithmetic and copies ran while one was open for 39% of the time, Pallas kernels for 0%

profile of v1, /device:TPU:96, one launch (start us, length us, event | category | flops | bytes accessed | tf_op | source)
XLA Modules:
  0.0 258.9 jit_solution(5359614774526087923)
XLA Ops:
  13.4 14.6 %all_gather.10 = bf16[1536,256]{1,0:T(8,128)(2,1)S(1)} all-gather(bf16[192,256]{1,0:T(8,128)(2,1)S(1)} %copy-done.12), channel_id=1, replica_groups=mesh['req'=8,'exp'=16] {'req'}, dimensions={0}, use_global_device_ids=true | all-gather | bytes 884736 | tf_op jit(solution)/shard_map/all_gather | solution.py:223
  29.0 4.6 %fusion.134 = (bf16[4,1024,256]{2,1,0:T(8,128)(2,1)}, bf16[4,1024,256]{2,1,0:T(8,128)(2,1)}) fusion(bf16[4,1024,512]{2,1,0:T(8,128)(2,1)} %param.28), kind=kLoop, calls=%fused_computation.179 | loop fusion | bytes 8388608 | tf_op jit(solution)/shard_map/vmap()/slice | solution.py:86
  35.5 3.0 %copy.161 = bf16[4,1024,256]{1,2,0:T(8,128)(2,1)S(1)} copy(bf16[4,1024,256]{2,1,0:T(8,128)(2,1)} %get-tuple-element.5) | data formatting | bytes 4194304
  38.5 4.0 %copy.164 = bf16[4,1024,256]{1,2,0:T(8,128)(2,1)} copy(bf16[4,1024,256]{2,1,0:T(8,128)(2,1)} %get-tuple-element.4) | data formatting | bytes 4194304
  44.6 2.6 %collective-permute-done.1 = bf16[192,256]{1,0:T(8,128)(2,1)S(1)} collective-permute-done((bf16[192,256]{1,0:T(8,128)(2,1)}, bf16[192,256]{1,0:T(8,128)(2,1)S(1)}, u32[]{:S(2)}, u32[]{:S(2)}) %collective-permute-start.1) | collective-permute-done | bytes 98336 | tf_op jit(solution)/shard_map/ppermute | solution.py:33
  63.2 2.6 %gather_fusion = bf16[8,192,256]{2,1,0:T(8,128)(2,1)} fusion(bf16[8,192,256]{2,1,0:T(8,128)(2,1)} %bitcast_dynamic-update-slice_fusion, s32[1024]{0:T(1024)S(1)} %pad_clamp_fusion), kind=kCustom, calls=%fused_computation | custom fusion | bytes 1572896 | tf_op jit(solution)/shard_map/gather | solution.py:42
  69.6 4.4 %fusion.140 = f32[256,1536]{0,1:T(8,128)S(1)} fusion(bf16[256,1536]{1,0:T(8,128)(2,1)S(1)} %fusion.38, bf16[1536,1536]{1,0:T(8,128)(2,1)} %all-gather.3.cloned.1.call-done), kind=kOutput, calls=%fused_computation.185 | convolution fusion | flops 1207959552 | bytes 7077888 | tf_op jit(solution)/shard_map/dot_general | solution.py:216
  80.0 3.1 %fusion.1 = f32[4,2,6,64]{3,2,1,0:T(8,128)S(1)} fusion(f32[4,2,64,6,1024]{4,2,3,1,0:T(8,128)S(1)} %get-tuple-element.25, f32[4,2,6,64]{3,2,1,0:T(8,128)S(1)} %max.25, pred[4,1024]{1,0:T(4,128)(4,1)S(1)} %iota_compare_fusion.8), kind=kLoop, calls=%fused_computation.7 | loop fusion | flops 12579840 | bytes 12611584 | tf_op jit(solution)/shard_map/vmap()/reduce_sum | solution.py:111
  84.8 4.1 %fusion.40 = bf16[4,64,2,6,128]{4,1,3,2,0:T(8,128)(2,1)S(1)} fusion(f32[4,2,128,6,64]{2,4,3,1,0:T(8,128)S(1)} %fusion.74, bf16[4,1024,2,128,1]{1,3,4,2,0:T(8,128)(2,1)S(1)} %bitcast.146, f32[4,2,64,6,1024]{4,2,3,1,0:T(8,128)S(1)} %get-tuple-element.25, f32[4,2,6,64]{3,2,1,0:T(8,128)S(1)} %add.137, f32[4,2,6,64]{3,2,1,0:T(8,128)S(1)} %max.25, ...), kind=kOutput, calls=%fused_computation.47 | convolution fusion | flops 821821440 | bytes 17068032 | tf_op jit(solution)/shard_map/vmap(gsij,jgd->igsd)/dot_general | solution.py:116
  90.0 4.1 %multiply_reduce_fusion.1 = (f32[128]{0:T(128)S(1)}, f32[128,1536]{1,0:T(8,128)S(1)}) fusion(bf16[128,1536]{1,0:T(8,128)(2,1)S(1)} %slice.81, bf16[1536,1536]{0,1:T(8,128)(2,1)} %all-gather.5.cloned.1.call-done, bf16[256,1536]{1,0:T(8,128)(2,1)S(1)} %copy-done.1), kind=kOutput, calls=%fused_computation.76 | convolution fusion | flops 605159296 | bytes 6291968 | tf_op jit(solution)/shard_map/dot_general | solution.py:244
  96.4 7.1 %all-to-all-start = ((bf16[16,2,24,1536]{3,2,1,0:T(8,128)(2,1)}), bf16[16,2,24,1536]{3,2,1,0:T(8,128)(2,1)}, u32[]{:S(2)}, u32[]{:S(2)}) async-start(bf16[16,2,24,1536]{3,2,1,0:T(8,128)(2,1)} %bitcast.26), calls=%async_computation | async-start | bytes 4718592 | tf_op jit(solution)/shard_map/all_to_all | solution.py:184
  104.2 4.1 %multiply_reduce_fusion = (f32[128]{0:T(128)S(1)}, f32[128,1536]{1,0:T(8,128)S(1)}) fusion(bf16[128,1536]{1,0:T(8,128)(2,1)S(1)} %slice.89, bf16[1536,1536]{0,1:T(8,128)(2,1)} %all-gather.5.cloned.1.call-done, bf16[256,1536]{1,0:T(8,128)(2,1)S(1)} %copy-done.1), kind=kOutput, calls=%fused_computation.74 | convolution fusion | flops 605159296 | bytes 6291968 | tf_op jit(solution)/shard_map/dot_general | solution.py:244
  110.6 27.4 %all-to-all-done = bf16[16,2,24,1536]{3,2,1,0:T(8,128)(2,1)} async-done(((bf16[16,2,24,1536]{3,2,1,0:T(8,128)(2,1)}), bf16[16,2,24,1536]{3,2,1,0:T(8,128)(2,1)}, u32[]{:S(2)}, u32[]{:S(2)}) %all-to-all-start) | async-done | bytes 2359328 | tf_op jit(solution)/shard_map/all_to_all | solution.py:184
  138.0 7.1 %all-to-all-start.2 = ((bf16[16,2,24,1536]{3,2,1,0:T(8,128)(2,1)}), bf16[16,2,24,1536]{3,2,1,0:T(8,128)(2,1)}, u32[]{:S(2)}, u32[]{:S(2)}) async-start(bf16[16,2,24,1536]{3,2,1,0:T(8,128)(2,1)} %bitcast.36), calls=%async_computation.2 | async-start | bytes 4718592 | tf_op jit(solution)/shard_map/all_to_all | solution.py:184
  145.2 6.5 %fusion.9 = f32[2,16,24,768]{3,2,1,0:T(8,128)} fusion(bf16[2,1536,768]{2,1,0:T(8,128)(2,1)} %param.24, bf16[16,2,24,1536]{3,2,1,0:T(8,128)(2,1)} %all-to-all-done), kind=kOutput, calls=%fused_computation.15 | convolution fusion | flops 1811939328 | bytes 9437184 | tf_op jit(solution)/shard_map/pekd,edf->pekf/dot_general | solution.py:162
  151.6 9.0 %fusion.25 = bf16[16,2,24,1536]{3,2,0,1:T(8,128)(2,1)S(1)} fusion(bf16[2,768,1536]{2,1,0:T(8,128)(2,1)} %param.25, f32[2,16,24,768]{3,2,1,0:T(8,128)} %fusion.9, bf16[2,1536,768]{2,1,0:T(8,128)(2,1)} %param.23, bf16[16,2,24,1536]{3,2,1,0:T(8,128)(2,1)} %all-to-all-done), kind=kOutput, calls=%fused_computation.27 | convolution fusion | flops 3626827776 | bytes 16515072 | tf_op jit(solution)/shard_map/pekf,efd->pekd/dot_general | solution.py:164
  162.3 16.8 %all-to-all-done.2 = bf16[16,2,24,1536]{3,2,1,0:T(8,128)(2,1)} async-done(((bf16[16,2,24,1536]{3,2,1,0:T(8,128)(2,1)}), bf16[16,2,24,1536]{3,2,1,0:T(8,128)(2,1)}, u32[]{:S(2)}, u32[]{:S(2)}) %all-to-all-start.2) | async-done | bytes 2359328 | tf_op jit(solution)/shard_map/all_to_all | solution.py:184
  179.0 3.9 %all-to-all-start.1 = ((bf16[16,2,24,1536]{3,2,1,0:T(8,128)(2,1)}), bf16[16,2,24,1536]{3,2,1,0:T(8,128)(2,1)S(1)}, u32[]{:S(2)}, u32[]{:S(2)}) async-start(bf16[16,2,24,1536]{3,2,1,0:T(8,128)(2,1)} %copy.136), calls=%async_computation.1 | async-start | bytes 4718592 | tf_op jit(solution)/shard_map/all_to_all | solution.py:189
  185.4 6.5 %fusion.7 = f32[2,16,24,768]{3,2,1,0:T(8,128)} fusion(bf16[2,1536,768]{2,1,0:T(8,128)(2,1)} %param.24, bf16[16,2,24,1536]{3,2,1,0:T(8,128)(2,1)} %all-to-all-done.2), kind=kOutput, calls=%fused_computation.13 | convolution fusion | flops 1811939328 | bytes 9437184 | tf_op jit(solution)/shard_map/pekd,edf->pekf/dot_general | solution.py:162
  191.9 10.4 %fusion.22 = bf16[16,2,24,1536]{3,2,0,1:T(8,128)(2,1)} fusion(bf16[2,768,1536]{2,1,0:T(8,128)(2,1)} %param.25, f32[2,16,24,768]{3,2,1,0:T(8,128)} %fusion.7, bf16[2,1536,768]{2,1,0:T(8,128)(2,1)} %param.23, bf16[16,2,24,1536]{3,2,1,0:T(8,128)(2,1)} %all-to-all-done.2), kind=kOutput, calls=%fused_computation.26 | convolution fusion | flops 3626827776 | bytes 16515072 | tf_op jit(solution)/shard_map/pekf,efd->pekd/dot_general | solution.py:164
  202.3 3.4 %copy.140 = bf16[16,2,24,1536]{3,2,1,0:T(8,128)(2,1)} copy(bf16[16,2,24,1536]{3,2,0,1:T(8,128)(2,1)} %fusion.22) | data formatting | bytes 4718592 | tf_op jit(solution)/shard_map/convert_element_type | solution.py:164
  205.7 7.8 %all-to-all-done.1 = bf16[16,2,24,1536]{3,2,1,0:T(8,128)(2,1)S(1)} async-done(((bf16[16,2,24,1536]{3,2,1,0:T(8,128)(2,1)}), bf16[16,2,24,1536]{3,2,1,0:T(8,128)(2,1)S(1)}, u32[]{:S(2)}, u32[]{:S(2)}) %all-to-all-start.1) | async-done | bytes 2359328 | tf_op jit(solution)/shard_map/all_to_all | solution.py:189
  213.6 4.4 %all-to-all-start.3 = ((bf16[16,2,24,1536]{3,2,1,0:T(8,128)(2,1)}), bf16[16,2,24,1536]{3,2,1,0:T(8,128)(2,1)}, u32[]{:S(2)}, u32[]{:S(2)}) async-start(bf16[16,2,24,1536]{3,2,1,0:T(8,128)(2,1)} %copy.140), calls=%async_computation.3 | async-start | bytes 4718592 | tf_op jit(solution)/shard_map/all_to_all | solution.py:189
  220.8 27.7 %all-to-all-done.3 = bf16[16,2,24,1536]{3,2,1,0:T(8,128)(2,1)} async-done(((bf16[16,2,24,1536]{3,2,1,0:T(8,128)(2,1)}), bf16[16,2,24,1536]{3,2,1,0:T(8,128)(2,1)}, u32[]{:S(2)}, u32[]{:S(2)}) %all-to-all-start.3) | async-done | bytes 2359328 | tf_op jit(solution)/shard_map/all_to_all | solution.py:189
  (134 shorter events, 55.0 us)
Async XLA Ops:
  7.2 6.0 %copy-start = (bf16[256,1536]{1,0:T(8,128)(2,1)S(1)}, bf16[256,1536]{1,0:T(8,128)(2,1)}, u32[]{:S(2)}) copy-start(bf16[256,1536]{1,0:T(8,128)(2,1)} %param.16) | copy-start | bytes 2359300
  7.2 6.2 %copy-start.12 = (bf16[192,256]{1,0:T(8,128)(2,1)S(1)}, bf16[192,256]{1,0:T(8,128)(2,1)}, u32[]{:S(2)}) copy-start(bf16[192,256]{1,0:T(8,128)(2,1)} %param.19) | copy-start | bytes 294916
  7.2 20.8 %copy-start.15 = (f32[1536]{0:T(1024)S(1)}, f32[1536]{0:T(1024)}, u32[]{:S(2)}) copy-start(f32[1536]{0:T(1024)} %param.17) | copy-start | bytes 18436
  7.2 62.4 %all-gather.3.cloned.1.call-start = ((), (), s32[]{:S(2)}) async-start(), calls=%async_computation.4 | async-start | bytes 5308416 | tf_op jit(solution)/shard_map/all_gather | solution.py:218
  7.9 81.8 %all-gather.5.cloned.1.call-start = ((), (), s32[]{:S(2)}) async-start(), calls=%async_computation.5 | async-start | bytes 5308416 | tf_op jit(solution)/shard_map/all_gather | solution.py:235
  8.0 35.0 %collective-permute-start = (bf16[192,256]{1,0:T(8,128)(2,1)}, bf16[192,256]{1,0:T(8,128)(2,1)}, u32[]{:S(2)}, u32[]{:S(2)}) collective-permute-start(bf16[192,256]{1,0:T(8,128)(2,1)} %param.20), channel_id=1, source_target_pairs={{0,16},{16,32},{32,48},{48,64},{64,80},{80,96},{96,112},{112,0},{1... | collective-permute-start | bytes 294920 | tf_op jit(solution)/shard_map/ppermute | solution.py:33
  8.0 39.2 %collective-permute-start.4 = (bf16[192,256]{1,0:T(8,128)(2,1)}, bf16[192,256]{1,0:T(8,128)(2,1)}, u32[]{:S(2)}, u32[]{:S(2)}) collective-permute-start(bf16[192,256]{1,0:T(8,128)(2,1)} %param.20), channel_id=1, source_target_pairs={{16,0},{32,16},{48,32},{64,48},{80,64},{96,80},{112,96},{0,112},{1... | collective-permute-start | bytes 294920 | tf_op jit(solution)/shard_map/ppermute | solution.py:35
  29.0 4.6 %copy-start.13 = (s32[256,4]{0,1:T(4,128)S(1)}, s32[256,4]{0,1:T(4,128)}, u32[]{:S(2)}) copy-start(s32[256,4]{0,1:T(4,128)} %param.26) | copy-start | bytes 12292
  29.0 5.7 %copy-start.17 = (s32[4]{0:T(128)S(1)}, s32[4]{0:T(128)}, u32[]{:S(2)}) copy-start(s32[4]{0:T(128)} %param.29) | copy-start | bytes 52
  43.0 4.3 %collective-permute-start.1 = (bf16[192,256]{1,0:T(8,128)(2,1)}, bf16[192,256]{1,0:T(8,128)(2,1)S(1)}, u32[]{:S(2)}, u32[]{:S(2)}) collective-permute-start(bf16[192,256]{1,0:T(8,128)(2,1)} %collective-permute-done), channel_id=1, source_target_pairs={{0,16},{16,32},{32,48},{48,64},{64,80},{80,96},{96,112},{112,0},{1... | collective-permute-start | bytes 294920 | tf_op jit(solution)/shard_map/ppermute | solution.py:33
  44.6 32.1 %copy-start.5 = (bf16[256,2,128]{2,0,1:T(8,128)(2,1)}, bf16[256,2,128]{2,0,1:T(8,128)(2,1)S(1)}, u32[]{:S(2)}) copy-start(bf16[256,2,128]{2,0,1:T(8,128)(2,1)S(1)} %pad_maximum_fusion.2) | copy-start | bytes 393220
  47.2 4.0 %collective-permute-start.2 = (bf16[192,256]{1,0:T(8,128)(2,1)S(1)}, bf16[192,256]{1,0:T(8,128)(2,1)S(1)}, u32[]{:S(2)}, u32[]{:S(2)}) collective-permute-start(bf16[192,256]{1,0:T(8,128)(2,1)S(1)} %collective-permute-done.1), channel_id=1, source_target_pairs={{0,16},{16,32},{32,48},{48,64},{64,80},{80,96},{96,112},{112,0},{1... | collective-permute-start | bytes 294920 | tf_op jit(solution)/shard_map/ppermute | solution.py:33
  47.3 4.3 %collective-permute-start.5 = (bf16[192,256]{1,0:T(8,128)(2,1)}, bf16[192,256]{1,0:T(8,128)(2,1)S(1)}, u32[]{:S(2)}, u32[]{:S(2)}) collective-permute-start(bf16[192,256]{1,0:T(8,128)(2,1)} %collective-permute-done.4), channel_id=1, source_target_pairs={{16,0},{32,16},{48,32},{64,48},{80,64},{96,80},{112,96},{0,112},{1... | collective-permute-start | bytes 294920 | tf_op jit(solution)/shard_map/ppermute | solution.py:35
  51.3 4.0 %collective-permute-start.3 = (bf16[192,256]{1,0:T(8,128)(2,1)S(1)}, bf16[192,256]{1,0:T(8,128)(2,1)S(1)}, u32[]{:S(2)}, u32[]{:S(2)}) collective-permute-start(bf16[192,256]{1,0:T(8,128)(2,1)S(1)} %collective-permute-done.2), channel_id=1, source_target_pairs={{0,16},{16,32},{32,48},{48,64},{64,80},{80,96},{96,112},{112,0},{1... | collective-permute-start | bytes 294920 | tf_op jit(solution)/shard_map/ppermute | solution.py:33
  51.5 11.0 %collective-permute-start.6 = (bf16[192,256]{1,0:T(8,128)(2,1)S(1)}, bf16[192,256]{1,0:T(8,128)(2,1)S(1)}, u32[]{:S(2)}, u32[]{:S(2)}) collective-permute-start(bf16[192,256]{1,0:T(8,128)(2,1)S(1)} %collective-permute-done.5), channel_id=1, source_target_pairs={{16,0},{32,16},{48,32},{64,48},{80,64},{96,80},{112,96},{0,112},{1... | collective-permute-start | bytes 294920 | tf_op jit(solution)/shard_map/ppermute | solution.py:35
  96.4 41.6 %all-to-all-start = ((bf16[16,2,24,1536]{3,2,1,0:T(8,128)(2,1)}), bf16[16,2,24,1536]{3,2,1,0:T(8,128)(2,1)}, u32[]{:S(2)}, u32[]{:S(2)}) async-start(bf16[16,2,24,1536]{3,2,1,0:T(8,128)(2,1)} %bitcast.26), calls=%async_computation | async-start | bytes 4718592 | tf_op jit(solution)/shard_map/all_to_all | solution.py:184
  108.3 29.7 %copy-start.2 = (f32[128,1536]{1,0:T(8,128)}, f32[128,1536]{1,0:T(8,128)S(1)}, u32[]{:S(2)}) copy-start(f32[128,1536]{1,0:T(8,128)S(1)} %get-tuple-element.29) | copy-start | bytes 2359300
  138.0 41.0 %all-to-all-start.2 = ((bf16[16,2,24,1536]{3,2,1,0:T(8,128)(2,1)}), bf16[16,2,24,1536]{3,2,1,0:T(8,128)(2,1)}, u32[]{:S(2)}, u32[]{:S(2)}) async-start(bf16[16,2,24,1536]{3,2,1,0:T(8,128)(2,1)} %bitcast.36), calls=%async_computation.2 | async-start | bytes 4718592 | tf_op jit(solution)/shard_map/all_to_all | solution.py:184
  162.3 20.7 %copy-start.6 = (bf16[256,2,128]{2,0,1:T(8,128)(2,1)S(1)}, bf16[256,2,128]{2,0,1:T(8,128)(2,1)}, u32[]{:S(2)}) copy-start(bf16[256,2,128]{2,0,1:T(8,128)(2,1)} %copy-done.5) | copy-start | bytes 393220
  162.3 21.6 %copy-start.18 = (s32[4]{0:T(128)S(1)}, s32[4]{0:T(128)}, u32[]{:S(2)}) copy-start(s32[4]{0:T(128)} %param.31) | copy-start | bytes 52
  179.0 34.5 %all-to-all-start.1 = ((bf16[16,2,24,1536]{3,2,1,0:T(8,128)(2,1)}), bf16[16,2,24,1536]{3,2,1,0:T(8,128)(2,1)S(1)}, u32[]{:S(2)}, u32[]{:S(2)}) async-start(bf16[16,2,24,1536]{3,2,1,0:T(8,128)(2,1)} %copy.136), calls=%async_computation.1 | async-start | bytes 4718592 | tf_op jit(solution)/shard_map/all_to_all | solution.py:189
  205.7 12.3 %copy-start.16 = (f32[256,4]{0,1:T(4,128)S(1)}, f32[256,4]{0,1:T(4,128)}, u32[]{:S(2)}) copy-start(f32[256,4]{0,1:T(4,128)} %param.27) | copy-start | bytes 12292
  213.6 34.9 %all-to-all-start.3 = ((bf16[16,2,24,1536]{3,2,1,0:T(8,128)(2,1)}), bf16[16,2,24,1536]{3,2,1,0:T(8,128)(2,1)}, u32[]{:S(2)}, u32[]{:S(2)}) async-start(bf16[16,2,24,1536]{3,2,1,0:T(8,128)(2,1)} %copy.140), calls=%async_computation.3 | async-start | bytes 4718592 | tf_op jit(solution)/shard_map/all_to_all | solution.py:189
  220.8 30.1 %copy-start.3 = (f32[128,1536]{1,0:T(8,128)S(1)}, f32[128,1536]{1,0:T(8,128)}, u32[]{:S(2)}) copy-start(f32[128,1536]{1,0:T(8,128)} %copy-done.2) | copy-start | bytes 2359300
  (8 other events, 16.3 us)
Sparse Core Ops, SparseCore 0:
  9.7 34.0 all-gather.2
  45.5 34.9 all-gather.4
